TPU v7x, 128 devices: a whole 4x4x4 slice. The times are simulated.
128 devices in a mesh: dp: 4 (over z_hi, core), mp: 32 (over x, y, z_lo).
Axes of the slice: x: 4, y: 4, z: 4 (z_hi: 2, z_lo: 2; z = z_hi * 2 + z_lo), core: 2. Of those that a mesh axis runs over, the one named last changes fastest.
Arguments:
- residual_input: bfloat16 [2048, 4608], P(('dp', 'mp')), may hold values from -6 to 6
- before_attention_gain: float32 [4608], replicated, may hold values from 0.25 to 1.75
- after_attention_gain: float32 [4608], replicated, may hold values from 0.25 to 1.75
- before_feedforward_gain: float32 [4608], replicated, may hold values from 0.25 to 1.75
- after_feedforward_gain: float32 [4608], replicated, may hold values from 0.25 to 1.75
- query_weight: bfloat16 [4608, 4096], P(None, 'mp'), may hold values from -0.09375 to 0.09375
- key_value_weight: bfloat16 [4608, 2, 32, 128], P(None, None, 'mp'), as said below
- output_weight: bfloat16 [4096, 4608], P('mp'), may hold values from -0.09375 to 0.09375
- gate_matrix: bfloat16 [4608, 20480], P(None, 'mp'), may hold values from -0.09375 to 0.09375
- up_matrix: bfloat16 [4608, 20480], P(None, 'mp'), may hold values from -0.09375 to 0.09375
- down_matrix: bfloat16 [20480, 4608], P('mp'), may hold values from -0.0390625 to 0.0390625
- key_value_cache: bfloat16 [256, 2, 32, 16, 128], P('dp', None, 'mp'), as said below
- projected_lowrank_left: bfloat16 [64, 4608, 16], P('mp'), may hold values from -0.09375 to 0.09375
- projected_lowrank_right: bfloat16 [64, 16, 3, 32, 128], P(None, None, None, 'mp'), as said below
- result_lowrank_left: bfloat16 [64, 4096, 16], P(None, 'mp'), may hold values from -0.09375 to 0.09375
- result_lowrank_right: bfloat16 [64, 16, 4608], P('mp'), may hold values from -1.5 to 1.5
- token_request: int32 [4, 512], P('dp'), may hold values from 0 to 7, never falling along the last dimension, each value on 1 to 256 neighbouring positions
- lowrank_choice_by_prompt: int32 [4, 8], P('dp'), may hold values from 0 to 63
- adapter_position: int32 [64], replicated, may hold values from 0 to 63, each once
- request_pages: int32 [4, 8, 4], replicated, may hold values from 0 to 255
Outputs:
- hidden_out: bfloat16 [2048, 4608], P(('dp', 'mp'))
- kv_new: bfloat16 [2048, 2, 32, 128], P('dp', None, 'mp')
Inputs may be any that keep to these rules, and one draw needn't show every extreme that they name: `key_value_weight`: query heads h and h2 with h // 2 == h2 // 2 have equal key and value weights: they share one key and value head. `key_value_cache`: query heads that share a key and value head have equal cached keys and values. `projected_lowrank_right`: the key and value parts of query heads that share a key and value head are equal. `token_request`: numbers never fall along a group; every request has at least one token. `adapter_position`: each slot once. `request_pages`: pages may repeat within and across requests.
All inputs are finite; a program needn't handle non-finite values.
Results may differ from a plain program's by a relative error of at most 0.035.
Values may be sent and summed in bfloat16 or wider, within the bound.
No kernel may reach another device: no remote copies, remote signals or barrier semaphores. Data moves between devices by JAX's collectives and lax.ppermute only.
A program may use at most 128 MiB of HBM per device.

v0:
```python
import math
import jax
import jax.numpy as jnp
from jax import lax
from jax.sharding import PartitionSpec as P

HIDDEN_BREADTH = 4608
ASKING_CHANNELS = 32
CHANNEL_LENGTH = 128
NUM_LOW_TERMS = 64
LOW_DIMENSION = 16
SHARD_PROMPTS = 8
PPR = 4
PAGE = 16
EPS = 1e-06
SOFTCAP = 50.0


def rms_scale(values, scaling):
    mean_square = jnp.mean(values * values, axis=-1, keepdims=True)
    return values * lax.rsqrt(mean_square + EPS) * scaling


def apply_rotary(values, token_positions):
    half_dim = values.shape[-1] // 2
    frequency = 10000.0 ** (-2.0 * jnp.arange(half_dim, dtype=jnp.float32) / values.shape[-1])
    angles = token_positions.astype(jnp.float32)[:, None] * frequency[None, :]
    cosine = jnp.cos(angles)[:, None, :]
    sine_part = jnp.sin(angles)[:, None, :]
    first_half = values[..., :half_dim]
    second_half = values[..., half_dim:]
    return jnp.concatenate(
        [
            first_half * cosine - second_half * sine_part,
            second_half * cosine + first_half * sine_part,
        ],
        axis=-1,
    )


def positions_of(segments):
    length = segments.shape[0]
    earlier = jnp.sum((segments[None, :] < segments[:, None]).astype(jnp.int32), axis=1)
    return PPR * PAGE + jnp.arange(length, dtype=jnp.int32) - earlier


def capped(scores):
    return SOFTCAP * jnp.tanh(scores / SOFTCAP)


def attend_local(query_rows, keys_new, fresh_values, keys_pre, values_pre, segments):
    scale_factor = 1.0 / math.sqrt(HIDDEN_BREADTH // ASKING_CHANNELS)
    length = segments.shape[0]
    prefix_owner = jnp.arange(keys_pre.shape[1], dtype=jnp.int32) // (PPR * PAGE)
    mask_pre = (prefix_owner[None, :] == segments[:, None])[None]
    ordinal = jnp.arange(length, dtype=jnp.int32)
    mask_new = ((segments[None, :] == segments[:, None]) & (ordinal[None, :] <= ordinal[:, None]))[
        None
    ]
    scores_pre = (
        jnp.einsum("thd,hjd->htj", query_rows, keys_pre, preferred_element_type=jnp.float32)
        * scale_factor
    )
    scores_new = (
        jnp.einsum("thd,uhd->htu", query_rows, keys_new, preferred_element_type=jnp.float32)
        * scale_factor
    )
    weight_pre = jnp.where(mask_pre, jnp.exp(capped(scores_pre)), 0.0)
    weight_new = jnp.where(mask_new, jnp.exp(capped(scores_new)), 0.0)
    totals = jnp.sum(weight_pre, axis=-1, keepdims=True) + jnp.sum(
        weight_new, axis=-1, keepdims=True
    )
    probs_pre = (weight_pre / totals).astype(jnp.bfloat16)
    probs_new = (weight_new / totals).astype(jnp.bfloat16)
    mixture = jnp.einsum("htj,hjd->thd", probs_pre, values_pre, preferred_element_type=jnp.float32)
    mixture = mixture + jnp.einsum(
        "htu,uhd->thd", probs_new, fresh_values, preferred_element_type=jnp.float32
    )
    return mixture.astype(jnp.bfloat16).reshape(length, -1)


def shards(
    residual_input,
    before_attention_gain,
    after_attention_gain,
    before_feedforward_gain,
    after_feedforward_gain,
    query_weight,
    key_value_weight,
    output_weight,
    gate_matrix,
    up_matrix,
    down_matrix,
    key_value_cache,
    projected_lowrank_left,
    projected_lowrank_right,
    result_lowrank_left,
    result_lowrank_right,
    token_request,
    lowrank_choice_by_prompt,
    adapter_position,
    request_pages,
):
    mp_index = lax.axis_index("mp")
    dp_index = lax.axis_index("dp")
    residual = residual_input.astype(jnp.float32)
    normed_rows = rms_scale(residual, before_attention_gain).astype(jnp.bfloat16)
    normalized_rows = lax.all_gather(normed_rows, "mp", axis=0, tiled=True)
    prompt_ordinal = normalized_rows.shape[0]
    channel_window = query_weight.shape[1] // CHANNEL_LENGTH
    query_rows = jnp.dot(normalized_rows, query_weight, preferred_element_type=jnp.float32).reshape(
        prompt_ordinal, channel_window, CHANNEL_LENGTH
    )
    key_value_rows = jnp.dot(
        normalized_rows,
        key_value_weight.reshape(HIDDEN_BREADTH, 2 * channel_window * CHANNEL_LENGTH),
        preferred_element_type=jnp.float32,
    ).reshape(prompt_ordinal, 2, channel_window, CHANNEL_LENGTH)
    segments = token_request[0]
    request_ids = lowrank_choice_by_prompt[0]
    request_range = jnp.arange(SHARD_PROMPTS, dtype=jnp.int32)
    membership = segments[:, None] == request_range[None, :]
    adapter_range = jnp.arange(NUM_LOW_TERMS, dtype=jnp.int32)
    token_adapter = jnp.sum(jnp.where(membership, request_ids[None, :], 0), axis=1)
    token_adapter_slot = jnp.sum(
        jnp.where(token_adapter[:, None] == adapter_range[None, :], adapter_position[None, :], 0),
        axis=1,
    )
    gathered_down = lax.all_gather(projected_lowrank_left, "mp", axis=0, tiled=True)
    request_slot = jnp.sum(
        jnp.where(request_ids[:, None] == adapter_range[None, :], adapter_position[None, :], 0),
        axis=1,
    )
    request_down = gathered_down[request_slot]
    request_factors = jnp.einsum(
        "td,rdk->trk", normalized_rows, request_down, preferred_element_type=jnp.float32
    )
    lowrank_source = jnp.sum(jnp.where(membership[:, :, None], request_factors, 0.0), axis=1)
    lowrank_source = lowrank_source.astype(jnp.bfloat16)
    choice_mask_table = membership.astype(jnp.bfloat16)
    broadened_lines = (choice_mask_table[:, :, None] * lowrank_source[:, None, :]).reshape(
        prompt_ordinal, SHARD_PROMPTS * LOW_DIMENSION
    )
    raised_result_lines = projected_lowrank_right[request_ids].reshape(
        SHARD_PROMPTS * LOW_DIMENSION, 3 * channel_window * CHANNEL_LENGTH
    )
    adapter_query_key_value = jnp.dot(
        broadened_lines, raised_result_lines, preferred_element_type=jnp.float32
    ).reshape(prompt_ordinal, 3, channel_window, CHANNEL_LENGTH)
    token_positions = positions_of(segments)
    rotary_queries = apply_rotary(
        query_rows + adapter_query_key_value[:, 0], token_positions
    ).astype(jnp.bfloat16)
    rotary_keys = apply_rotary(
        key_value_rows[:, 0] + adapter_query_key_value[:, 1], token_positions
    ).astype(jnp.bfloat16)
    fresh_values = (key_value_rows[:, 1] + adapter_query_key_value[:, 2]).astype(jnp.bfloat16)
    kv_new = jnp.stack([rotary_keys, fresh_values], axis=1)
    own_pages = lax.dynamic_index_in_dim(request_pages, dp_index, 0, keepdims=False).reshape(
        SHARD_PROMPTS * PPR
    )
    whole_pool = lax.all_gather(key_value_cache, "dp", axis=0, tiled=True)
    chosen = whole_pool[own_pages]
    keys_pre = jnp.transpose(chosen[:, 0], (1, 0, 2, 3)).reshape(
        channel_window, SHARD_PROMPTS * PPR * PAGE, CHANNEL_LENGTH
    )
    values_pre = jnp.transpose(chosen[:, 1], (1, 0, 2, 3)).reshape(
        channel_window, SHARD_PROMPTS * PPR * PAGE, CHANNEL_LENGTH
    )
    attended = attend_local(
        rotary_queries, rotary_keys, fresh_values, keys_pre, values_pre, segments
    )
    request_output_down = result_lowrank_left[request_ids]
    request_output_factors = jnp.einsum(
        "tc,rck->trk", attended, request_output_down, preferred_element_type=jnp.float32
    )
    output_adapter_piece = jnp.sum(
        jnp.where(membership[:, :, None], request_output_factors, 0.0), axis=1
    )
    result_lowrank_source = lax.psum(output_adapter_piece.astype(jnp.bfloat16), "mp")
    result_seat_lines = result_lowrank_right.shape[0]
    output_slots = mp_index * result_seat_lines + jnp.arange(result_seat_lines, dtype=jnp.int32)
    resident_here = (token_adapter_slot[:, None] == output_slots[None, :]).astype(jnp.bfloat16)
    broadened_result = (resident_here[:, :, None] * result_lowrank_source[:, None, :]).reshape(
        prompt_ordinal, result_seat_lines * LOW_DIMENSION
    )
    raised_window = result_lowrank_right.reshape(result_seat_lines * LOW_DIMENSION, HIDDEN_BREADTH)
    attn_sum = lax.psum_scatter(
        (
            jnp.dot(attended, output_weight, preferred_element_type=jnp.float32)
            + jnp.dot(broadened_result, raised_window, preferred_element_type=jnp.float32)
        ).astype(jnp.bfloat16),
        "mp",
        scatter_dimension=0,
        tiled=True,
    ).astype(jnp.float32)
    after_attn = (residual + rms_scale(attn_sum, after_attention_gain)).astype(jnp.bfloat16)
    normed_ffw = rms_scale(after_attn.astype(jnp.float32), before_feedforward_gain).astype(
        jnp.bfloat16
    )
    piece = lax.all_gather(normed_ffw, "mp", axis=0, tiled=True)
    gated = jnp.dot(piece, gate_matrix, preferred_element_type=jnp.float32)
    upward = jnp.dot(piece, up_matrix, preferred_element_type=jnp.float32)
    hidden = (jax.nn.gelu(gated, approximate=True) * upward).astype(jnp.bfloat16)
    ffw_sum = lax.psum_scatter(
        jnp.dot(hidden, down_matrix, preferred_element_type=jnp.float32).astype(jnp.bfloat16),
        "mp",
        scatter_dimension=0,
        tiled=True,
    ).astype(jnp.float32)
    hidden_out = (
        after_attn.astype(jnp.float32) + rms_scale(ffw_sum, after_feedforward_gain)
    ).astype(jnp.bfloat16)
    return (hidden_out, kv_new)


def solution(mesh):
    return jax.shard_map(
        shards,
        mesh=mesh,
        in_specs=(
            P(("dp", "mp"), None),
            P(),
            P(),
            P(),
            P(),
            P(None, "mp"),
            P(None, None, "mp", None),
            P("mp", None),
            P(None, "mp"),
            P(None, "mp"),
            P("mp", None),
            P("dp", None, "mp", None, None),
            P("mp", None, None),
            P(None, None, None, "mp", None),
            P(None, "mp", None),
            P("mp", None, None),
            P("dp", None),
            P("dp", None),
            P(),
            P(),
        ),
        out_specs=(P(("dp", "mp"), None), P("dp", None, "mp", None)),
        check_vma=False,
    )
```

profile of v0, /device:TPU:0, one launch (start us, length us, event | category | flops | bytes accessed | tf_op | source)
XLA Modules:
  0.0 1112.8 jit_solution(17951339612052338414)
XLA Ops:
  7.2 0.7 all-gather.5.cloned.1.call-update
  8.0 1.1 fusion.31
  9.0 1.7 fusion.33
  10.8 0.7 all-gather.9.cloned.1.call-update
  11.5 0.7 constant_dynamic-slice_fusion
  12.2 0.1 copy.46
  12.3 0.1 reshape.488
  12.4 0.7 fusion.73
  13.1 2.1 gather_fusion.3
  15.2 1.7 gather_fusion.2
  16.9 0.8 copy.48
  17.7 2.0 copy.60
  19.7 2.5 copy.50
  22.3 0.2 select_reduce_fusion.4
  22.5 0.1 select_reduce_fusion.3
  22.6 0.1 select_reduce_fusion.2
  22.7 0.2 convert_reduce_fusion
  23.0 15.9 %all-gather.5.cloned.1.call-done = bf16[256,2,1,16,128]{4,3,2,1,0:T(8,128)(2,1)} async-done(((bf16[64,2,1,16,128]{4,3,2,1,0:T(8,128)(2,1)}), bf16[256,2,1,16,128]{4,3,2,1,0:T(8,128)(2,1)}) %all-gather.5.cloned.1.call-update) | async-done | bytes 2097168 | tf_op jit(solution)/shard_map/all_gather | solution.py:162
  38.9 2.2 gather_fusion
  41.2 157.9 %all-gather.7.cloned.1.call-done = bf16[512,4608]{1,0:T(8,128)(2,1)} async-done(((bf16[16,4608]{1,0:T(8,128)(2,1)}), bf16[512,4608]{1,0:T(8,128)(2,1)}) %all-gather.7.cloned.1.call-update) | async-done | bytes 4718608 | tf_op jit(solution)/shard_map/all_gather | solution.py:108
  199.1 4.5 fusion.19
  203.6 207.7 %all-gather.9.cloned.1.call-done = bf16[64,4608,16]{1,2,0:T(8,128)(2,1)} async-done(((bf16[2,4608,16]{1,2,0:T(8,128)(2,1)}), bf16[64,4608,16]{1,2,0:T(8,128)(2,1)}) %all-gather.9.cloned.1.call-update) | async-done | bytes 9437200 | tf_op jit(solution)/shard_map/all_gather | solution.py:129
  411.2 4.3 gather_fusion.1
  415.6 4.1 fusion.84
  419.8 0.2 convolution_bitcast_fusion
  420.0 0.1 fusion.39
  420.1 1.7 fusion.22
  421.8 0.6 fusion.54
  422.4 0.5 fusion.82
  422.9 0.5 fusion.83
  423.4 0.3 fusion.26
  423.7 0.2 fusion.24
  423.9 0.2 fusion.86
  424.2 157.2 %psum.7 = bf16[512,16]{0,1:T(8,128)(2,1)S(1)} all-reduce(bf16[512,16]{0,1:T(8,128)(2,1)S(1)} %select_reduce_fusion), channel_id=1, replica_groups=mesh['dp'=4,'mp'=32] {'mp'}, use_global_device_ids=true, to_apply=%region_9.10 | all-reduce | flops 8192 | bytes 32768 | tf_op jit(solution)/shard_map/psum | solution.py:180
  581.4 1.4 fusion.63
  582.8 3.5 fusion
  586.4 165.2 %reduce-scatter.3.cloned.1.call-done = bf16[16,4608]{1,0:T(8,128)(2,1)} async-done(((bf16[512,4608]{1,0:T(8,128)(2,1)}), bf16[16,4608]{1,0:T(8,128)(2,1)}) %reduce-scatter.3.cloned.1.call-update) | async-done | bytes 147472 | tf_op jit(solution)/shard_map/reduce_scatter | solution.py:188
  751.6 1.1 fusion.27
  752.7 1.2 fusion.35
  753.9 0.8 fusion.37
  754.7 0.2 reduce-scatter.5.cloned.1.call-start
  754.9 154.9 %all-gather.11.cloned.1.call-done = bf16[512,4608]{1,0:T(8,128)(2,1)} async-done(((bf16[16,4608]{1,0:T(8,128)(2,1)}), bf16[512,4608]{1,0:T(8,128)(2,1)}) %all-gather.11.cloned.1.call-update) | async-done | bytes 4718608 | tf_op jit(solution)/shard_map/all_gather | solution.py:201
  909.8 7.4 fusion.85
  917.2 14.2 %convolution_convert_fusion = bf16[512,4608]{1,0:T(8,128)(2,1)} fusion(bf16[640,4608]{1,0:T(8,128)(2,1)} %param.30, bf16[512,4608]{1,0:T(8,128)(2,1)} %all-gather.11.cloned.1.call-done, bf16[4608,640]{1,0:T(8,128)(2,1)} %param.29, f32[512,640]{1,0:T(8,128)S(1)} %fusion.85), kind=kOutput, calls=%fused_computation.6 | convolution fusion | flops 6045433856 | bytes 22544384 | tf_op jit(solution)/shard_map/dot_general | solution.py:206
  931.5 0.9 copy.52
  932.4 170.8 %reduce-scatter.5.cloned.1.call-done = bf16[16,4608]{1,0:T(8,128)(2,1)} async-done(((bf16[512,4608]{1,0:T(8,128)(2,1)}), bf16[16,4608]{1,0:T(8,128)(2,1)}) %reduce-scatter.5.cloned.1.call-update) | async-done | bytes 147472 | tf_op jit(solution)/shard_map/reduce_scatter | solution.py:205
  1103.2 1.1 fusion.29
  1104.3 1.7 fusion.38
  (63 shorter events, 0.7 us)
Async XLA Ops:
  7.2 575.7 %copy-start = (bf16[128,4608]{1,0:T(8,128)(2,1)S(1)}, bf16[128,4608]{1,0:T(8,128)(2,1)}, u32[]{:S(2)}) copy-start(bf16[128,4608]{1,0:T(8,128)(2,1)} %param.27) | copy-start | bytes 3538948
  7.2 31.8 %all-gather.5.cloned.1.call-start = ((), (), s32[]{:S(2)}) async-start(), calls=%async_computation.2 | async-start | bytes 2621440 | tf_op jit(solution)/shard_map/all_gather | solution.py:162
  7.9 191.1 %all-gather.7.cloned.1.call-start = ((), (), s32[]{:S(2)}) async-start(), calls=%async_computation.3 | async-start | bytes 4866048 | tf_op jit(solution)/shard_map/all_gather | solution.py:108
  10.7 400.5 %all-gather.9.cloned.1.call-start = ((), (), s32[]{:S(2)}) async-start(), calls=%async_computation.4 | async-start | bytes 9732096 | tf_op jit(solution)/shard_map/all_gather | solution.py:129
  11.5 740.1 %reduce-scatter.3.cloned.1.call-start = ((), (), s32[]{:S(2)}) async-start(), calls=%async_computation.5 | async-start | bytes 4866048 | tf_op jit(solution)/shard_map/reduce_scatter | solution.py:188
  17.7 4.6 copy-start.11
  17.7 4.6 copy-start.12
  17.7 4.8 copy-start.7
  415.5 4.2 copy-start.5
  415.5 4.6 slice-start
  415.6 4.6 copy-start.4
  415.6 4.6 slice-start.1
  422.9 1.0 copy-start.2
  423.4 158.0 %copy-start.6 = (bf16[2,16,4608]{2,1,0:T(8,128)(2,1)S(1)}, bf16[2,16,4608]{2,1,0:T(8,128)(2,1)}, u32[]{:S(2)}) copy-start(bf16[2,16,4608]{2,1,0:T(8,128)(2,1)} %param.35) | copy-start | bytes 884740
  586.4 166.3 %copy-start.3 = (bf16[16,4608]{1,0:T(8,128)(2,1)S(1)}, bf16[16,4608]{1,0:T(8,128)(2,1)}, u32[]{:S(2)}) copy-start(bf16[16,4608]{1,0:T(8,128)(2,1)} %param.20) | copy-start | bytes 442372
  586.4 166.3 %copy-start.8 = (f32[4608]{0:T(1024)S(1)}, f32[4608]{0:T(1024)}, u32[]{:S(2)}) copy-start(f32[4608]{0:T(1024)} %param.22) | copy-start | bytes 55300
  586.4 167.5 %copy-start.9 = (f32[4608]{0:T(1024)S(1)}, f32[4608]{0:T(1024)}, u32[]{:S(2)}) copy-start(f32[4608]{0:T(1024)} %param.23) | copy-start | bytes 55300
  586.4 323.4 %all-gather.11.cloned.1.call-start = ((), (), s32[]{:S(2)}) async-start(), calls=%async_computation.6 | async-start | bytes 4866048 | tf_op jit(solution)/shard_map/all_gather | solution.py:201
  754.7 348.5 %reduce-scatter.5.cloned.1.call-start = ((), (), s32[]{:S(2)}) async-start(), calls=%async_computation.7 | async-start | bytes 4866048 | tf_op jit(solution)/shard_map/reduce_scatter | solution.py:205
  917.2 188.7 %copy-start.1 = (bf16[128,4608]{1,0:T(8,128)(2,1)S(1)}, bf16[128,4608]{1,0:T(8,128)(2,1)}, u32[]{:S(2)}) copy-start(bf16[128,4608]{1,0:T(8,128)(2,1)} %param.27) | copy-start | bytes 3538948
  931.5 172.8 %copy-start.10 = (f32[4608]{0:T(1024)S(1)}, f32[4608]{0:T(1024)}, u32[]{:S(2)}) copy-start(f32[4608]{0:T(1024)} %param.24) | copy-start | bytes 55300
Sparse Core Ops, SparseCore 0:
  9.7 29.2 all-gather.4
  41.1 157.8 all-gather.6
  200.7 210.4 all-gather.8
  586.5 165.0 reduce-scatter.2
  754.8 154.9 all-gather.10
  931.6 171.5 reduce-scatter.4
where the time goes:
time: 1110 us
  waiting for transfers between devices  874 us (79%)
  blocking collectives  157 us (14%)
  matrix products  38.8 us (3%)
  local copies, waits for them, and re-layouts  17.5 us (2%)
  between operations  14.5 us (1%)
    all_gather x1, waiting for transfers between devices, shards(): lax.all_gather(projected_lowrank_left, 'mp', axis=0, tiled=True)  208 us
    reduce_scatter x1, waiting for transfers between devices, shards(): lax.psum_scatter(jnp.dot(hidden, down_matrix, preferred_element_type=jnp....  171 us
    reduce_scatter x1, waiting for transfers between devices, shards(): lax.psum_scatter((jnp.dot(attended, output_weight, preferred_element_type...  165 us
    all_gather x1, waiting for transfers between devices, shards(): normalized_rows = lax.all_gather(normed_rows, 'mp', axis=0, tiled=True)  158 us
    psum x1, blocking collectives, shards(): lax.psum(output_adapter_piece.astype(jnp.bfloat16), 'mp')  157 us
    all_gather x1, waiting for transfers between devices, shards(): piece = lax.all_gather(normed_ffw, 'mp', axis=0, tiled=True)  155 us
  transfers between devices with their start and end apart: 6, of which 6 were waited for; matrix products, arithmetic and copies ran while one was open for 2% of the time, Pallas kernels for 0%

commit v1 on v0

--- a/solution.py
+++ b/solution.py
@@ -177,7 +177,8 @@
     output_adapter_piece = jnp.sum(
         jnp.where(membership[:, :, None], request_output_factors, 0.0), axis=1
     )
-    result_lowrank_source = lax.psum(output_adapter_piece.astype(jnp.bfloat16), "mp")
+    my_tile = output_adapter_piece.astype(jnp.bfloat16)
+    result_lowrank_source = lax.all_gather(my_tile, "mp").sum(axis=0)
     result_seat_lines = result_lowrank_right.shape[0]
     output_slots = mp_index * result_seat_lines + jnp.arange(result_seat_lines, dtype=jnp.int32)
     resident_here = (token_adapter_slot[:, None] == output_slots[None, :]).astype(jnp.bfloat16)

time: 1110 us -> 1040 us (0.937)
  blocking collectives: 157 us -> 83.4 us
    psum x1 -> x0, blocking collectives: 157 us -> none  [shards(): lax.psum(output_adapter_piece.astype(jnp.bfloat16), 'mp')]
    all_gather x0 -> x1, blocking collectives: none -> 83.4 us  [shards(): result_lowrank_source = lax.all_gather(my_tile, 'mp').sum(axis=0)]
where the time goes in v1:
time: 1040 us
  waiting for transfers between devices  873 us (84%)
  blocking collectives  83.4 us (8%)
  matrix products  38.8 us (4%)
  local copies, waits for them, and re-layouts  17.6 us (2%)
  between operations  14.5 us (1%)
  other arithmetic  10.8 us (1%)
    all_gather x1, waiting for transfers between devices, shards(): lax.all_gather(projected_lowrank_left, 'mp', axis=0, tiled=True)  208 us
    reduce_scatter x1, waiting for transfers between devices, shards(): lax.psum_scatter(jnp.dot(hidden, down_matrix, preferred_element_type=jnp....  171 us
    reduce_scatter x1, waiting for transfers between devices, shards(): lax.psum_scatter((jnp.dot(attended, output_weight, preferred_element_type...  165 us
    all_gather x1, waiting for transfers between devices, shards(): normalized_rows = lax.all_gather(normed_rows, 'mp', axis=0, tiled=True)  158 us
    all_gather x1, waiting for transfers between devices, shards(): piece = lax.all_gather(normed_ffw, 'mp', axis=0, tiled=True)  154 us
    all_gather x1, blocking collectives, shards(): result_lowrank_source = lax.all_gather(my_tile, 'mp').sum(axis=0)  83.4 us
  transfers between devices with their start and end apart: 6, of which 6 were waited for; matrix products, arithmetic and copies ran while one was open for 2% of the time, Pallas kernels for 0%

profile of v1, /device:TPU:0, one launch (start us, length us, event | category | flops | bytes accessed | tf_op | source)
XLA Modules:
  0.0 1038.3 jit_solution(6048571489283260224)
XLA Ops:
  7.2 0.7 all-gather.6.cloned.1.call-update
  8.0 1.1 fusion.31
  9.0 1.7 fusion.33
  10.8 0.7 all-gather.10.cloned.1.call-update
  11.5 0.7 constant_dynamic-slice_fusion
  12.4 0.7 fusion.73
  13.1 2.1 gather_fusion.3
  15.2 1.7 gather_fusion.2
  16.9 0.8 copy.50
  17.7 2.0 copy.63
  19.7 2.5 copy.52
  22.3 0.2 select_reduce_fusion.4
  22.5 0.1 select_reduce_fusion.3
  22.6 0.1 select_reduce_fusion.2
  22.7 0.2 convert_reduce_fusion
  23.0 15.9 %all-gather.6.cloned.1.call-done = bf16[256,2,1,16,128]{4,3,2,1,0:T(8,128)(2,1)} async-done(((bf16[64,2,1,16,128]{4,3,2,1,0:T(8,128)(2,1)}), bf16[256,2,1,16,128]{4,3,2,1,0:T(8,128)(2,1)}) %all-gather.6.cloned.1.call-update) | async-done | bytes 2097168 | tf_op jit(solution)/shard_map/all_gather | solution.py:162
  38.9 2.2 gather_fusion
  41.2 157.9 %all-gather.8.cloned.1.call-done = bf16[512,4608]{1,0:T(8,128)(2,1)} async-done(((bf16[16,4608]{1,0:T(8,128)(2,1)}), bf16[512,4608]{1,0:T(8,128)(2,1)}) %all-gather.8.cloned.1.call-update) | async-done | bytes 4718608 | tf_op jit(solution)/shard_map/all_gather | solution.py:108
  199.1 4.5 fusion.19
  203.6 207.7 %all-gather.10.cloned.1.call-done = bf16[64,4608,16]{1,2,0:T(8,128)(2,1)} async-done(((bf16[2,4608,16]{1,2,0:T(8,128)(2,1)}), bf16[64,4608,16]{1,2,0:T(8,128)(2,1)}) %all-gather.10.cloned.1.call-update) | async-done | bytes 9437200 | tf_op jit(solution)/shard_map/all_gather | solution.py:129
  411.2 4.3 gather_fusion.1
  415.6 4.1 fusion.84
  419.8 0.2 convolution_bitcast_fusion
  420.0 0.1 fusion.39
  420.1 1.7 fusion.22
  421.8 0.6 fusion.54
  422.4 0.5 fusion.82
  422.9 0.5 fusion.83
  423.4 0.3 fusion.26
  423.7 0.2 fusion.24
  423.9 0.2 fusion.86
  424.2 83.4 %all-gather = bf16[16384,16]{0,1:T(8,128)(2,1)S(1)} all-gather(bf16[512,16]{0,1:T(8,128)(2,1)S(1)} %select_reduce_fusion), channel_id=2, replica_groups=mesh['dp'=4,'mp'=32] {'mp'}, dimensions={0}, use_global_device_ids=true | all-gather | bytes 540672 | tf_op jit(solution)/shard_map/all_gather | solution.py:181
  507.5 0.2 copy.60
  507.7 0.2 bitcast_reduce_fusion
  507.8 1.4 fusion.63
  509.3 3.5 fusion
  512.9 165.3 %reduce-scatter.3.cloned.1.call-done = bf16[16,4608]{1,0:T(8,128)(2,1)} async-done(((bf16[512,4608]{1,0:T(8,128)(2,1)}), bf16[16,4608]{1,0:T(8,128)(2,1)}) %reduce-scatter.3.cloned.1.call-update) | async-done | bytes 147472 | tf_op jit(solution)/shard_map/reduce_scatter | solution.py:189
  678.2 1.1 fusion.27
  679.3 1.2 fusion.35
  680.4 0.8 fusion.37
  681.2 0.2 reduce-scatter.5.cloned.1.call-start
  681.5 154.0 %all-gather.12.cloned.1.call-done = bf16[512,4608]{1,0:T(8,128)(2,1)} async-done(((bf16[16,4608]{1,0:T(8,128)(2,1)}), bf16[512,4608]{1,0:T(8,128)(2,1)}) %all-gather.12.cloned.1.call-update) | async-done | bytes 4718608 | tf_op jit(solution)/shard_map/all_gather | solution.py:202
  835.4 7.4 fusion.85
  842.9 14.2 %convolution_convert_fusion = bf16[512,4608]{1,0:T(8,128)(2,1)} fusion(bf16[640,4608]{1,0:T(8,128)(2,1)} %param.30, bf16[512,4608]{1,0:T(8,128)(2,1)} %all-gather.12.cloned.1.call-done, bf16[4608,640]{1,0:T(8,128)(2,1)} %param.29, f32[512,640]{1,0:T(8,128)S(1)} %fusion.85), kind=kOutput, calls=%fused_computation.6 | convolution fusion | flops 6045433856 | bytes 22544384 | tf_op jit(solution)/shard_map/dot_general | solution.py:207
  857.1 0.9 copy.54
  858.0 170.6 %reduce-scatter.5.cloned.1.call-done = bf16[16,4608]{1,0:T(8,128)(2,1)} async-done(((bf16[512,4608]{1,0:T(8,128)(2,1)}), bf16[16,4608]{1,0:T(8,128)(2,1)}) %reduce-scatter.5.cloned.1.call-update) | async-done | bytes 147472 | tf_op jit(solution)/shard_map/reduce_scatter | solution.py:206
  1028.7 1.1 fusion.29
  1029.7 1.7 fusion.38
  (65 shorter events, 0.9 us)
Async XLA Ops:
  7.2 502.1 %copy-start = (bf16[128,4608]{1,0:T(8,128)(2,1)S(1)}, bf16[128,4608]{1,0:T(8,128)(2,1)}, u32[]{:S(2)}) copy-start(bf16[128,4608]{1,0:T(8,128)(2,1)} %param.27) | copy-start | bytes 3538948
  7.2 31.8 %all-gather.6.cloned.1.call-start = ((), (), s32[]{:S(2)}) async-start(), calls=%async_computation.2 | async-start | bytes 2621440 | tf_op jit(solution)/shard_map/all_gather | solution.py:162
  7.9 191.1 %all-gather.8.cloned.1.call-start = ((), (), s32[]{:S(2)}) async-start(), calls=%async_computation.3 | async-start | bytes 4866048 | tf_op jit(solution)/shard_map/all_gather | solution.py:108
  10.7 400.5 %all-gather.10.cloned.1.call-start = ((), (), s32[]{:S(2)}) async-start(), calls=%async_computation.4 | async-start | bytes 9732096 | tf_op jit(solution)/shard_map/all_gather | solution.py:129
  11.5 666.7 %reduce-scatter.3.cloned.1.call-start = ((), (), s32[]{:S(2)}) async-start(), calls=%async_computation.5 | async-start | bytes 4866048 | tf_op jit(solution)/shard_map/reduce_scatter | solution.py:189
  17.7 4.6 copy-start.11
  17.7 4.6 copy-start.12
  17.7 4.8 copy-start.7
  415.5 4.2 copy-start.5
  415.5 4.6 slice-start
  415.6 4.6 copy-start.4
  415.6 4.6 slice-start.1
  422.9 1.0 copy-start.2
  423.4 84.4 %copy-start.6 = (bf16[2,16,4608]{2,1,0:T(8,128)(2,1)S(1)}, bf16[2,16,4608]{2,1,0:T(8,128)(2,1)}, u32[]{:S(2)}) copy-start(bf16[2,16,4608]{2,1,0:T(8,128)(2,1)} %param.35) | copy-start | bytes 884740
  512.8 166.4 %copy-start.3 = (bf16[16,4608]{1,0:T(8,128)(2,1)S(1)}, bf16[16,4608]{1,0:T(8,128)(2,1)}, u32[]{:S(2)}) copy-start(bf16[16,4608]{1,0:T(8,128)(2,1)} %param.20) | copy-start | bytes 442372
  512.8 166.4 %copy-start.8 = (f32[4608]{0:T(1024)S(1)}, f32[4608]{0:T(1024)}, u32[]{:S(2)}) copy-start(f32[4608]{0:T(1024)} %param.22) | copy-start | bytes 55300
  512.8 167.6 %copy-start.9 = (f32[4608]{0:T(1024)S(1)}, f32[4608]{0:T(1024)}, u32[]{:S(2)}) copy-start(f32[4608]{0:T(1024)} %param.23) | copy-start | bytes 55300
  512.8 322.6 %all-gather.12.cloned.1.call-start = ((), (), s32[]{:S(2)}) async-start(), calls=%async_computation.6 | async-start | bytes 4866048 | tf_op jit(solution)/shard_map/all_gather | solution.py:202
  681.2 347.4 %reduce-scatter.5.cloned.1.call-start = ((), (), s32[]{:S(2)}) async-start(), calls=%async_computation.7 | async-start | bytes 4866048 | tf_op jit(solution)/shard_map/reduce_scatter | solution.py:206
  842.8 188.6 %copy-start.1 = (bf16[128,4608]{1,0:T(8,128)(2,1)S(1)}, bf16[128,4608]{1,0:T(8,128)(2,1)}, u32[]{:S(2)}) copy-start(bf16[128,4608]{1,0:T(8,128)(2,1)} %param.27) | copy-start | bytes 3538948
  857.1 172.6 %copy-start.10 = (f32[4608]{0:T(1024)S(1)}, f32[4608]{0:T(1024)}, u32[]{:S(2)}) copy-start(f32[4608]{0:T(1024)} %param.24) | copy-start | bytes 55300
Sparse Core Ops, SparseCore 0:
  9.7 29.2 all-gather.5
  41.1 157.8 all-gather.7
  200.7 210.4 all-gather.9
  513.0 165.1 reduce-scatter.2
  681.3 154.0 all-gather.11
  857.2 171.3 reduce-scatter.4
